TPU v7x, 256 devices: a whole 4x4x8 slice. The times are simulated.
256 devices in a mesh: tm: 8 (over x, core), space: 32 (over y, z).
Axes of the slice: x: 4, y: 4, z: 8, core: 2. Of those that a mesh axis runs over, the one named last changes fastest.
Arguments:
- snapshots: bfloat16 [2016, 5, 64, 8, 128], P('tm', None, 'space'), may hold values from -6 to 6
- picks: int32 [1792], P('tm'), may hold values from 0 to 251, as said below
- basis: bfloat16 [32, 5, 64, 8, 128], P(None, None, 'space'), may hold values from -0.01953125 to 0.01953125
- kappa: float32 [5, 64, 8, 128], P(None, 'space'), may hold values from 0.03 to 0.16
Outputs:
- coefficients: float32 [1792, 32], P('tm')
- factor: float32 [561, 561], replicated
Inputs may be any that keep to these rules, and one draw needn't show every extreme that they name: `picks`: within each time group's 224 consecutive entries the indices are distinct, and 0 and 251 both occur.
All inputs are finite; a program needn't handle non-finite values.
Results may differ from a plain program's by a relative error of at most 0.0003.
Values may be sent and summed in bfloat16 or wider, within the bound.
No kernel may reach another device: no remote copies, remote signals or barrier semaphores. Data moves between devices by JAX's collectives and lax.ppermute only.
A program may use at most 64 MiB of HBM per device.

v0:
```python
import jax
import jax.numpy as jnp
import numpy as np
from jax import lax
from jax.sharding import PartitionSpec as P

BLOCK = 32


def with_halo(block, sides, width):
    for axis, dim in sides:
        count = lax.axis_size(axis)
        forward = [(i, i + 1) for i in range(count - 1)]
        backward = [(target, source) for source, target in forward]
        low = lax.ppermute(
            lax.slice_in_dim(block, block.shape[dim] - width, None, axis=dim), axis, forward
        )
        high = lax.ppermute(lax.slice_in_dim(block, 0, width, axis=dim), axis, backward)
        block = jnp.concatenate([low, block, high], axis=dim)
    return block


def smooth_block(padded, kappa):
    widened = jnp.pad(padded.astype(jnp.float32), ((0, 0), (0, 0), (0, 0), (1, 1), (1, 1)))
    center = widened[:, :, 1:-1, 1:-1, 1:-1]
    beside = widened[:, :, 2:, 1:-1, 1:-1] + widened[:, :, :-2, 1:-1, 1:-1]
    beside = beside + widened[:, :, 1:-1, 2:, 1:-1] + widened[:, :, 1:-1, :-2, 1:-1]
    beside = beside + widened[:, :, 1:-1, 1:-1, 2:] + widened[:, :, 1:-1, 1:-1, :-2]
    return center + kappa * (beside - 6.0 * center)


def project(filtered, basis_flat):
    flat = filtered.reshape(filtered.shape[0], -1)
    return lax.dot_general(
        flat,
        basis_flat,
        (((1,), (1,)), ((), ())),
        precision=lax.Precision.HIGHEST,
        preferred_element_type=jnp.float32,
    )


def expand(coeffs):
    count = coeffs.shape[1]
    first, second = np.triu_indices(count)
    quad = coeffs[:, first] * coeffs[:, second]
    ones = jnp.ones((coeffs.shape[0], 1), coeffs.dtype)
    return jnp.concatenate([ones, coeffs, quad], axis=1)


def body(snapshots, picks, basis, kappa):
    modes_wide = basis.astype(jnp.float32)
    basis_flat = modes_wide.reshape(basis.shape[0], -1)
    count = picks.shape[0]
    rounds = count // BLOCK
    results = []
    for which in range(rounds):
        block = jnp.take(snapshots, picks[which * BLOCK : (which + 1) * BLOCK], axis=0)
        padded = with_halo(block, (("space", 2),), 1)
        filtered = smooth_block(padded, kappa)
        partial_sum = project(filtered, basis_flat)
        results.append(lax.psum(partial_sum, "space"))
    joined = jnp.concatenate(results, axis=0)
    features = expand(joined)
    total_rows = count * lax.axis_size("tm")
    local_gram = jnp.dot(features.T, features, precision=lax.Precision.HIGHEST)
    gram = lax.psum(local_gram, "tm") / total_rows
    factor = jnp.linalg.cholesky(gram).T
    return (joined, factor)


def solution(mesh):
    in_specs = (
        P("tm", None, "space", None, None),
        P("tm"),
        P(None, None, "space", None, None),
        P(None, "space", None, None),
    )
    out_specs = (P("tm", None), P())
    return jax.shard_map(body, mesh=mesh, in_specs=in_specs, out_specs=out_specs, check_vma=False)
```

profile of v0, /device:TPU:8, one launch (start us, length us, event | category | flops | bytes accessed | tf_op | source)
XLA Modules:
  0.0 454.6 jit_solution(4578447315816021161)
XLA Ops:
  8.3 3.1 gather_fusion.3
  13.4 3.8 collective-permute-start.2
  17.2 5.7 %collective-permute-start.3 = (bf16[32,5,1,8,128]{4,3,2,1,0:T(8,128)(2,1)}, bf16[32,5,1,8,128]{4,3,2,1,0:T(8,128)(2,1)}, u32[]{:S(2)}, u32[]{:S(2)}) collective-permute-start(bf16[32,5,1,8,128]{4,3,2,1,0:T(8,128)(2,1)} %get-tuple-element.39), channel_id=1, source_target_pairs={{1,0},{2,1},{3,2},{4,3},{5,4},{6,5},{7,6},{8,7},{9,8},{10,9},{11,1... | collective-permute-start | bytes 983048 | tf_op jit(solution)/shard_map/ppermute | solution.py:18
  23.0 3.1 gather_fusion.4
  28.1 1.9 collective-permute-start.4
  30.0 6.0 %collective-permute-start.5 = (bf16[32,5,1,8,128]{4,3,2,1,0:T(8,128)(2,1)}, bf16[32,5,1,8,128]{4,3,2,1,0:T(8,128)(2,1)}, u32[]{:S(2)}, u32[]{:S(2)}) collective-permute-start(bf16[32,5,1,8,128]{4,3,2,1,0:T(8,128)(2,1)} %get-tuple-element.37), channel_id=1, source_target_pairs={{1,0},{2,1},{3,2},{4,3},{5,4},{6,5},{7,6},{8,7},{9,8},{10,9},{11,1... | collective-permute-start | bytes 983048 | tf_op jit(solution)/shard_map/ppermute | solution.py:18
  36.0 3.1 gather_fusion.5
  41.1 1.9 collective-permute-start.6
  43.1 3.1 gather_fusion.8
  47.3 3.1 gather_fusion.6
  51.6 3.1 gather_fusion.7
  55.8 3.9 gather_fusion.2
  62.0 6.0 %collective-permute-start.7 = (bf16[32,5,1,8,128]{4,3,2,1,0:T(8,128)(2,1)S(1)}, bf16[32,5,1,8,128]{4,3,2,1,0:T(8,128)(2,1)S(1)}, u32[]{:S(2)}, u32[]{:S(2)}) collective-permute-start(bf16[32,5,1,8,128]{4,3,2,1,0:T(8,128)(2,1)S(1)} %copy-done.14), channel_id=1, source_target_pairs={{1,0},{2,1},{3,2},{4,3},{5,4},{6,5},{7,6},{8,7},{9,8},{10,9},{11,1... | collective-permute-start | bytes 983048 | tf_op jit(solution)/shard_map/ppermute | solution.py:18
  68.1 2.1 collective-permute-start.12
  70.1 1.4 maximum_convert_fusion.1
  71.6 6.0 %collective-permute-start.13 = (bf16[32,5,1,8,128]{4,3,2,1,0:T(8,128)(2,1)S(1)}, bf16[32,5,1,8,128]{4,3,2,1,0:T(8,128)(2,1)S(1)}, u32[]{:S(2)}, u32[]{:S(2)}) collective-permute-start(bf16[32,5,1,8,128]{4,3,2,1,0:T(8,128)(2,1)S(1)} %copy-done.13), channel_id=1, source_target_pairs={{1,0},{2,1},{3,2},{4,3},{5,4},{6,5},{7,6},{8,7},{9,8},{10,9},{11,1... | collective-permute-start | bytes 983048 | tf_op jit(solution)/shard_map/ppermute | solution.py:18
  77.6 2.1 collective-permute-start.8
  79.7 1.4 maximum_convert_fusion.2
  81.1 6.0 %collective-permute-start.9 = (bf16[32,5,1,8,128]{4,3,2,1,0:T(8,128)(2,1)}, bf16[32,5,1,8,128]{4,3,2,1,0:T(8,128)(2,1)}, u32[]{:S(2)}, u32[]{:S(2)}) collective-permute-start(bf16[32,5,1,8,128]{4,3,2,1,0:T(8,128)(2,1)} %get-tuple-element.33), channel_id=1, source_target_pairs={{1,0},{2,1},{3,2},{4,3},{5,4},{6,5},{7,6},{8,7},{9,8},{10,9},{11,1... | collective-permute-start | bytes 983048 | tf_op jit(solution)/shard_map/ppermute | solution.py:18
  87.2 1.9 collective-permute-start.10
  90.5 6.0 %collective-permute-start.11 = (bf16[32,5,1,8,128]{4,3,2,1,0:T(8,128)(2,1)}, bf16[32,5,1,8,128]{4,3,2,1,0:T(8,128)(2,1)}, u32[]{:S(2)}, u32[]{:S(2)}) collective-permute-start(bf16[32,5,1,8,128]{4,3,2,1,0:T(8,128)(2,1)} %get-tuple-element.31), channel_id=1, source_target_pairs={{1,0},{2,1},{3,2},{4,3},{5,4},{6,5},{7,6},{8,7},{9,8},{10,9},{11,1... | collective-permute-start | bytes 983048 | tf_op jit(solution)/shard_map/ppermute | solution.py:18
  96.5 1.9 collective-permute-start
  98.8 4.4 fusion.49
  103.2 2.5 fusion.67
  106.9 6.3 %collective-permute-start.1 = (bf16[32,5,1,8,128]{4,3,2,1,0:T(8,128)(2,1)S(1)}, bf16[32,5,1,8,128]{4,3,2,1,0:T(8,128)(2,1)S(1)}, u32[]{:S(2)}, u32[]{:S(2)}) collective-permute-start(bf16[32,5,1,8,128]{4,3,2,1,0:T(8,128)(2,1)S(1)} %get-tuple-element.41), channel_id=1, source_target_pairs={{1,0},{2,1},{3,2},{4,3},{5,4},{6,5},{7,6},{8,7},{9,8},{10,9},{11,1... | collective-permute-start | bytes 983048 | tf_op jit(solution)/shard_map/ppermute | solution.py:18
  113.3 1.4 maximum_convert_fusion.4
  115.9 1.5 maximum_convert_fusion.5
  119.9 2.2 fusion.42
  125.6 122.1 %all-reduce.8 = (f32[32,32]{1,0:T(8,128)S(1)}, f32[32,32]{1,0:T(8,128)S(1)}, f32[32,32]{1,0:T(8,128)S(1)}, f32[32,32]{1,0:T(8,128)S(1)}, f32[32,32]{1,0:T(8,128)...) all-reduce(f32[32,32]{1,0:T(8,128)S(1)} %fusion.64, ...), channel_id=1, replica_groups=mesh['tm'=8,'space'=32] {'space'}, use_global_device_ids=true, to_apply=%region_0.0 | all-reduce | flops 7168 | bytes 57344 | tf_op jit(solution)/shard_map/psum | solution.py:62
  248.4 2.1 gather_fusion
  250.5 2.3 gather_fusion.1
  252.9 2.8 fusion.85
  255.8 73.9 %all-reduce.11.cloned.1.call-done = f32[561,561]{0,1:T(8,128)} async-done(((f32[561,561]{0,1:T(8,128)}), f32[561,561]{0,1:T(8,128)}) %all-reduce.11.cloned.1.call-update) | async-done | bytes 1258900 | tf_op jit(solution)/shard_map/psum | solution.py:67
  329.7 2.6 broadcast_multiply_fusion
  332.3 3.1 copy.53
  335.3 1.6 fusion
  338.0 11.7 %cholesky.134 = f32[128,128]{1,0:T(8,128)S(1)} custom-call(f32[128,128]{1,0:T(8,128)S(1)} %cholesky.346), custom_call_target="Cholesky" | custom-call | tf_op jit(solution)/shard_map/jit(cholesky)/cholesky | solution.py:68
  349.9 9.8 %custom-call.35 = f32[1,128,128]{1,2,0:T(8,128)S(1)} custom-call(f32[1,128,128]{2,1,0:T(8,128)S(1)} %get-tuple-element.52), custom_call_target="InvertDiagBlocksLowerTriangular" | custom-call | tf_op jit(solution)/shard_map/jit(cholesky)/cholesky | solution.py:68
  359.7 1.4 constant_dynamic-update-slice_fusion.3
  361.1 1.5 convolution_subtract_fusion
  362.6 12.1 %cholesky.274 = f32[128,128]{1,0:T(8,128)S(1)} custom-call(f32[128,128]{1,0:T(8,128)S(1)} %cholesky.350), custom_call_target="Cholesky" | custom-call | tf_op jit(solution)/shard_map/jit(cholesky)/cholesky | solution.py:68
  376.0 9.8 %custom-call.36 = f32[1,128,128]{1,2,0:T(8,128)S(1)} custom-call(f32[1,128,128]{2,1,0:T(8,128)S(1)} %get-tuple-element.49), custom_call_target="InvertDiagBlocksLowerTriangular" | custom-call | tf_op jit(solution)/shard_map/jit(cholesky)/cholesky | solution.py:68
  387.6 11.7 %cholesky.295 = f32[128,128]{1,0:T(8,128)S(1)} custom-call(f32[128,128]{1,0:T(8,128)S(1)} %cholesky.355), custom_call_target="Cholesky" | custom-call | tf_op jit(solution)/shard_map/jit(cholesky)/cholesky | solution.py:68
  400.0 9.8 %custom-call.37 = f32[1,128,128]{1,2,0:T(8,128)S(1)} custom-call(f32[1,128,128]{2,1,0:T(8,128)S(1)} %get-tuple-element.46), custom_call_target="InvertDiagBlocksLowerTriangular" | custom-call | tf_op jit(solution)/shard_map/jit(cholesky)/cholesky | solution.py:68
  411.5 11.9 %cholesky.314 = f32[128,128]{1,0:T(8,128)S(1)} custom-call(f32[128,128]{1,0:T(8,128)S(1)} %cholesky.360), custom_call_target="Cholesky" | custom-call | tf_op jit(solution)/shard_map/jit(cholesky)/cholesky | solution.py:68
  424.1 9.8 %custom-call.38 = f32[1,128,128]{1,2,0:T(8,128)S(1)} custom-call(f32[1,128,128]{2,1,0:T(8,128)S(1)} %get-tuple-element.43), custom_call_target="InvertDiagBlocksLowerTriangular" | custom-call | tf_op jit(solution)/shard_map/jit(cholesky)/cholesky | solution.py:68
  435.2 4.5 cholesky.334
  444.6 3.0 copy.54
  (116 shorter events, 33.5 us)
Async XLA Ops:
  7.2 96.1 %copy-start = (bf16[32,5,2,8,128]{4,3,2,1,0:T(8,128)(2,1)S(1)}, bf16[32,5,2,8,128]{4,3,2,1,0:T(8,128)(2,1)}, u32[]{:S(2)}) copy-start(bf16[32,5,2,8,128]{4,3,2,1,0:T(8,128)(2,1)} %param.12) | copy-start | bytes 1966084
  7.2 322.5 %all-reduce.11.cloned.1.call-start = ((), (), s32[]{:S(2)}) async-start(), calls=%async_computation | async-start | bytes 2908160 | tf_op jit(solution)/shard_map/psum | solution.py:67
  11.5 0.8 copy-start.6
  13.4 48.6 %collective-permute-start.2 = (bf16[32,5,1,8,128]{4,3,2,1,0:T(8,128)(2,1)}, bf16[32,5,1,8,128]{4,3,2,1,0:T(8,128)(2,1)}, u32[]{:S(2)}, u32[]{:S(2)}) collective-permute-start(bf16[32,5,1,8,128]{4,3,2,1,0:T(8,128)(2,1)} %get-tuple-element.38), channel_id=1, source_target_pairs={{0,1},{1,2},{2,3},{3,4},{4,5},{5,6},{6,7},{7,8},{8,9},{9,10},{10,1... | collective-permute-start | bytes 983048 | tf_op jit(solution)/shard_map/ppermute | solution.py:15
  17.2 50.8 %collective-permute-start.3 = (bf16[32,5,1,8,128]{4,3,2,1,0:T(8,128)(2,1)}, bf16[32,5,1,8,128]{4,3,2,1,0:T(8,128)(2,1)}, u32[]{:S(2)}, u32[]{:S(2)}) collective-permute-start(bf16[32,5,1,8,128]{4,3,2,1,0:T(8,128)(2,1)} %get-tuple-element.39), channel_id=1, source_target_pairs={{1,0},{2,1},{3,2},{4,3},{5,4},{6,5},{7,6},{8,7},{9,8},{10,9},{11,1... | collective-permute-start | bytes 983048 | tf_op jit(solution)/shard_map/ppermute | solution.py:18
  26.2 0.9 copy-start.2
  28.1 43.5 %collective-permute-start.4 = (bf16[32,5,1,8,128]{4,3,2,1,0:T(8,128)(2,1)}, bf16[32,5,1,8,128]{4,3,2,1,0:T(8,128)(2,1)}, u32[]{:S(2)}, u32[]{:S(2)}) collective-permute-start(bf16[32,5,1,8,128]{4,3,2,1,0:T(8,128)(2,1)} %get-tuple-element.36), channel_id=1, source_target_pairs={{0,1},{1,2},{2,3},{3,4},{4,5},{5,6},{6,7},{7,8},{8,9},{9,10},{10,1... | collective-permute-start | bytes 983048 | tf_op jit(solution)/shard_map/ppermute | solution.py:15
  30.0 47.6 %collective-permute-start.5 = (bf16[32,5,1,8,128]{4,3,2,1,0:T(8,128)(2,1)}, bf16[32,5,1,8,128]{4,3,2,1,0:T(8,128)(2,1)}, u32[]{:S(2)}, u32[]{:S(2)}) collective-permute-start(bf16[32,5,1,8,128]{4,3,2,1,0:T(8,128)(2,1)} %get-tuple-element.37), channel_id=1, source_target_pairs={{1,0},{2,1},{3,2},{4,3},{5,4},{6,5},{7,6},{8,7},{9,8},{10,9},{11,1... | collective-permute-start | bytes 983048 | tf_op jit(solution)/shard_map/ppermute | solution.py:18
  39.3 0.8 copy-start.4
  41.1 40.0 %collective-permute-start.6 = (bf16[32,5,1,8,128]{4,3,2,1,0:T(8,128)(2,1)}, bf16[32,5,1,8,128]{4,3,2,1,0:T(8,128)(2,1)}, u32[]{:S(2)}, u32[]{:S(2)}) collective-permute-start(bf16[32,5,1,8,128]{4,3,2,1,0:T(8,128)(2,1)} %get-tuple-element.34), channel_id=1, source_target_pairs={{0,1},{1,2},{2,3},{3,4},{4,5},{5,6},{6,7},{7,8},{8,9},{9,10},{10,1... | collective-permute-start | bytes 983048 | tf_op jit(solution)/shard_map/ppermute | solution.py:15
  59.7 2.2 copy-start.17
  59.7 2.2 copy-start.18
  59.7 2.2 copy-start.14
  59.7 8.3 %copy-start.15 = (bf16[32,5,1,8,128]{4,3,2,1,0:T(8,128)(2,1)S(1)}, bf16[32,5,1,8,128]{4,3,2,1,0:T(8,128)(2,1)}, u32[]{:S(2)}) copy-start(bf16[32,5,1,8,128]{4,3,2,1,0:T(8,128)(2,1)} %get-tuple-element.28) | copy-start | bytes 983044
  59.7 10.4 %copy-start.7 = (bf16[32,5,2,8,128]{4,3,2,1,0:T(8,128)(2,1)S(1)}, bf16[32,5,2,8,128]{4,3,2,1,0:T(8,128)(2,1)}, u32[]{:S(2)}) copy-start(bf16[32,5,2,8,128]{4,3,2,1,0:T(8,128)(2,1)} %copy-done.6) | copy-start | bytes 1966084
  62.0 25.2 %collective-permute-start.7 = (bf16[32,5,1,8,128]{4,3,2,1,0:T(8,128)(2,1)S(1)}, bf16[32,5,1,8,128]{4,3,2,1,0:T(8,128)(2,1)S(1)}, u32[]{:S(2)}, u32[]{:S(2)}) collective-permute-start(bf16[32,5,1,8,128]{4,3,2,1,0:T(8,128)(2,1)S(1)} %copy-done.14), channel_id=1, source_target_pairs={{1,0},{2,1},{3,2},{4,3},{5,4},{6,5},{7,6},{8,7},{9,8},{10,9},{11,1... | collective-permute-start | bytes 983048 | tf_op jit(solution)/shard_map/ppermute | solution.py:18
  68.1 3.5 copy-start.13
  68.1 11.6 %copy-start.3 = (bf16[32,5,2,8,128]{4,3,2,1,0:T(8,128)(2,1)S(1)}, bf16[32,5,2,8,128]{4,3,2,1,0:T(8,128)(2,1)}, u32[]{:S(2)}) copy-start(bf16[32,5,2,8,128]{4,3,2,1,0:T(8,128)(2,1)} %copy-done.2) | copy-start | bytes 1966084
  68.1 22.4 %collective-permute-start.12 = (bf16[32,5,1,8,128]{4,3,2,1,0:T(8,128)(2,1)S(1)}, bf16[32,5,1,8,128]{4,3,2,1,0:T(8,128)(2,1)S(1)}, u32[]{:S(2)}, u32[]{:S(2)}) collective-permute-start(bf16[32,5,1,8,128]{4,3,2,1,0:T(8,128)(2,1)S(1)} %copy-done.15), channel_id=1, source_target_pairs={{0,1},{1,2},{2,3},{3,4},{4,5},{5,6},{6,7},{7,8},{8,9},{9,10},{10,1... | collective-permute-start | bytes 983048 | tf_op jit(solution)/shard_map/ppermute | solution.py:15
  71.6 24.9 %collective-permute-start.13 = (bf16[32,5,1,8,128]{4,3,2,1,0:T(8,128)(2,1)S(1)}, bf16[32,5,1,8,128]{4,3,2,1,0:T(8,128)(2,1)S(1)}, u32[]{:S(2)}, u32[]{:S(2)}) collective-permute-start(bf16[32,5,1,8,128]{4,3,2,1,0:T(8,128)(2,1)S(1)} %copy-done.13), channel_id=1, source_target_pairs={{1,0},{2,1},{3,2},{4,3},{5,4},{6,5},{7,6},{8,7},{9,8},{10,9},{11,1... | collective-permute-start | bytes 983048 | tf_op jit(solution)/shard_map/ppermute | solution.py:18
  77.6 11.5 %copy-start.5 = (bf16[32,5,2,8,128]{4,3,2,1,0:T(8,128)(2,1)S(1)}, bf16[32,5,2,8,128]{4,3,2,1,0:T(8,128)(2,1)}, u32[]{:S(2)}) copy-start(bf16[32,5,2,8,128]{4,3,2,1,0:T(8,128)(2,1)} %copy-done.4) | copy-start | bytes 1966084
  77.6 29.3 %collective-permute-start.8 = (bf16[32,5,1,8,128]{4,3,2,1,0:T(8,128)(2,1)}, bf16[32,5,1,8,128]{4,3,2,1,0:T(8,128)(2,1)}, u32[]{:S(2)}, u32[]{:S(2)}) collective-permute-start(bf16[32,5,1,8,128]{4,3,2,1,0:T(8,128)(2,1)} %get-tuple-element.32), channel_id=1, source_target_pairs={{0,1},{1,2},{2,3},{3,4},{4,5},{5,6},{6,7},{7,8},{8,9},{9,10},{10,1... | collective-permute-start | bytes 983048 | tf_op jit(solution)/shard_map/ppermute | solution.py:15
  81.1 32.2 %collective-permute-start.9 = (bf16[32,5,1,8,128]{4,3,2,1,0:T(8,128)(2,1)}, bf16[32,5,1,8,128]{4,3,2,1,0:T(8,128)(2,1)}, u32[]{:S(2)}, u32[]{:S(2)}) collective-permute-start(bf16[32,5,1,8,128]{4,3,2,1,0:T(8,128)(2,1)} %get-tuple-element.33), channel_id=1, source_target_pairs={{1,0},{2,1},{3,2},{4,3},{5,4},{6,5},{7,6},{8,7},{9,8},{10,9},{11,1... | collective-permute-start | bytes 983048 | tf_op jit(solution)/shard_map/ppermute | solution.py:18
  87.2 28.7 %collective-permute-start.10 = (bf16[32,5,1,8,128]{4,3,2,1,0:T(8,128)(2,1)}, bf16[32,5,1,8,128]{4,3,2,1,0:T(8,128)(2,1)}, u32[]{:S(2)}, u32[]{:S(2)}) collective-permute-start(bf16[32,5,1,8,128]{4,3,2,1,0:T(8,128)(2,1)} %get-tuple-element.30), channel_id=1, source_target_pairs={{0,1},{1,2},{2,3},{3,4},{4,5},{5,6},{6,7},{7,8},{8,9},{9,10},{10,1... | collective-permute-start | bytes 983048 | tf_op jit(solution)/shard_map/ppermute | solution.py:15
  90.5 25.4 %collective-permute-start.11 = (bf16[32,5,1,8,128]{4,3,2,1,0:T(8,128)(2,1)}, bf16[32,5,1,8,128]{4,3,2,1,0:T(8,128)(2,1)}, u32[]{:S(2)}, u32[]{:S(2)}) collective-permute-start(bf16[32,5,1,8,128]{4,3,2,1,0:T(8,128)(2,1)} %get-tuple-element.31), channel_id=1, source_target_pairs={{1,0},{2,1},{3,2},{4,3},{5,4},{6,5},{7,6},{8,7},{9,8},{10,9},{11,1... | collective-permute-start | bytes 983048 | tf_op jit(solution)/shard_map/ppermute | solution.py:18
  96.5 2.3 copy-start.16
  96.5 22.1 %collective-permute-start = (bf16[32,5,1,8,128]{4,3,2,1,0:T(8,128)(2,1)}, bf16[32,5,1,8,128]{4,3,2,1,0:T(8,128)(2,1)}, u32[]{:S(2)}, u32[]{:S(2)}) collective-permute-start(bf16[32,5,1,8,128]{4,3,2,1,0:T(8,128)(2,1)} %get-tuple-element.40), channel_id=1, source_target_pairs={{0,1},{1,2},{2,3},{3,4},{4,5},{5,6},{6,7},{7,8},{8,9},{9,10},{10,1... | collective-permute-start | bytes 983048 | tf_op jit(solution)/shard_map/ppermute | solution.py:15
  103.2 2.6 copy-start.11
  106.9 7.8 %copy-start.10 = (f32[32,5,2,8,128]{4,3,2,1,0:T(8,128)S(1)}, f32[32,5,2,8,128]{4,3,2,1,0:T(8,128)}, u32[]{:S(2)}) copy-start(f32[32,5,2,8,128]{4,3,2,1,0:T(8,128)} %get-tuple-element.56) | copy-start | bytes 3932164
  106.9 11.6 %collective-permute-start.1 = (bf16[32,5,1,8,128]{4,3,2,1,0:T(8,128)(2,1)S(1)}, bf16[32,5,1,8,128]{4,3,2,1,0:T(8,128)(2,1)S(1)}, u32[]{:S(2)}, u32[]{:S(2)}) collective-permute-start(bf16[32,5,1,8,128]{4,3,2,1,0:T(8,128)(2,1)S(1)} %get-tuple-element.41), channel_id=1, source_target_pairs={{1,0},{2,1},{3,2},{4,3},{5,4},{6,5},{7,6},{8,7},{9,8},{10,9},{11,1... | collective-permute-start | bytes 983048 | tf_op jit(solution)/shard_map/ppermute | solution.py:18
  115.9 1.6 copy-start.9
  248.3 4.6 %copy-start.1 = (f32[224,32]{0,1:T(8,128)}, f32[224,32]{0,1:T(8,128)S(1)}, u32[]{:S(2)}) copy-start(f32[224,32]{0,1:T(8,128)S(1)} %concatenate.34) | copy-start | bytes 86020
  332.3 3.1 copy-start.8
  336.9 1.1 copy-start.12
Sparse Core Ops, SparseCore 0:
  255.9 73.7 all-reduce.10
where the time goes:
time: 463 us; the launch traced here: 455 us
  blocking collectives  122 us (26%)
  other arithmetic  118 us (25%)
  waiting for transfers between devices  74 us (16%)
  starting transfers between devices  57.9 us (13%)
  local copies, waits for them, and re-layouts  44.4 us (10%)
  matrix products  19.7 us (4%)
  between operations  18.1 us (4%)
    psum x1, blocking collectives, body(): results.append(lax.psum(partial_sum, 'space'))  122 us
    another operation x19, other arithmetic, body(): factor = jnp.linalg.cholesky(gram).T  94.5 us
    psum x1, waiting for transfers between devices, body(): gram = lax.psum(local_gram, 'tm') / total_rows  73.9 us
    ppermute x7, starting transfers between devices, with_halo(): lax.ppermute(lax.slice_in_dim(block, 0, width, axis=dim), axis, backward)  42.2 us
    gather x7, local copies, waits for them, and re-layouts, body(): jnp.take(snapshots, picks[which * BLOCK:(which + 1) * BLOCK], axis=0)  22.8 us
    ppermute x7, starting transfers between devices, with_halo(): lax.ppermute(lax.slice_in_dim(block, block.shape[dim] - width, None, axis...  15.6 us
    dot_general x7, matrix products, project(): lax.dot_general(flat, basis_flat, (((1,), (1,)), ((), ())), precision=lax...  9.39 us
  transfers between devices with their start and end apart: 15, of which 1 were waited for; matrix products, arithmetic and copies ran while one was open for 10% of the time, Pallas kernels for 0%

commit v1 on v0

--- a/solution.py
+++ b/solution.py
@@ -59,7 +59,7 @@
         padded = with_halo(block, (("space", 2),), 1)
         filtered = smooth_block(padded, kappa)
         partial_sum = project(filtered, basis_flat)
-        results.append(lax.psum(partial_sum, "space"))
+        results.append(jnp.sum(lax.all_gather(partial_sum, "space"), axis=0))
     joined = jnp.concatenate(results, axis=0)
     features = expand(joined)
     total_rows = count * lax.axis_size("tm")

time: 463 us -> 684 us (1.48)
  blocking collectives: 122 us -> 344 us
    all_gather x0 -> x7, blocking collectives: none -> 344 us  [body(): results.append(jnp.sum(lax.all_gather(partial_sum, 'space'), axis=0))]
    psum x1 -> x0, blocking collectives: 122 us -> none  [body(): results.append(lax.psum(partial_sum, 'space'))]
    psum x1, waiting for transfers between devices: 73.9 us -> 66.1 us  [body(): gram = lax.psum(local_gram, 'tm') / total_rows]
  transfers between devices with their start and end apart: 15 -> 15, of which waited for: 1 -> 2; matrix products, arithmetic and copies ran while one was open for 10% -> 7% of each run, Pallas kernels for 0% -> 0%
where the time goes in v1:
time: 684 us; the launch traced here: 674 us
  blocking collectives  344 us (50%)
  other arithmetic  121 us (18%)
  waiting for transfers between devices  68.6 us (10%)
  starting transfers between devices  55.2 us (8%)
  local copies, waits for them, and re-layouts  46.6 us (7%)
  matrix products  21 us (3%)
  between operations  18 us (3%)
    all_gather x7, blocking collectives, body(): results.append(jnp.sum(lax.all_gather(partial_sum, 'space'), axis=0))  344 us
    another operation x19, other arithmetic, body(): factor = jnp.linalg.cholesky(gram).T  94.5 us
    psum x1, waiting for transfers between devices, body(): gram = lax.psum(local_gram, 'tm') / total_rows  66.1 us
    ppermute x7, starting transfers between devices, with_halo(): lax.ppermute(lax.slice_in_dim(block, 0, width, axis=dim), axis, backward)  39.6 us
    gather x7, local copies, waits for them, and re-layouts, body(): jnp.take(snapshots, picks[which * BLOCK:(which + 1) * BLOCK], axis=0)  22.8 us
    ppermute x7, starting transfers between devices, with_halo(): lax.ppermute(lax.slice_in_dim(block, block.shape[dim] - width, None, axis...  15.6 us
  transfers between devices with their start and end apart: 15, of which 2 were waited for; matrix products, arithmetic and copies ran while one was open for 7% of the time, Pallas kernels for 0%

profile of v1, /device:TPU:8, one launch (start us, length us, event | category | flops | bytes accessed | tf_op | source)
XLA Modules:
  0.0 674.2 jit_solution(17459542336797214501)
XLA Ops:
  8.3 3.1 gather_fusion.3
  13.4 3.8 collective-permute-start.2
  17.2 5.7 collective-permute-start.3
  23.0 3.1 gather_fusion.4
  30.0 6.0 collective-permute-start.5
  36.0 3.1 gather_fusion.5
  41.1 1.9 collective-permute-start.6
  43.0 3.1 gather_fusion.8
  47.3 3.1 gather_fusion.6
  51.6 3.1 gather_fusion.7
  55.8 3.9 gather_fusion.2
  62.7 6.0 collective-permute-start.7
  68.8 2.1 collective-permute-start.12
  72.3 6.0 collective-permute-start.13
  78.3 2.1 collective-permute-start.8
  81.8 6.0 collective-permute-start.9
  87.9 1.9 collective-permute-start.10
  91.1 6.0 collective-permute-start.11
  97.2 1.9 collective-permute-start
  99.5 4.4 fusion.49
  103.9 2.5 fusion.67
  108.9 50.4 %all-gather.1 = f32[1024,32]{1,0:T(8,128)S(1)} all-gather(f32[32,32]{1,0:T(8,128)S(1)} %fusion.67), channel_id=3, replica_groups=mesh['tm'=8,'space'=32] {'space'}, dimensions={0}, use_global_device_ids=true | all-gather | bytes 135168 | tf_op jit(solution)/shard_map/all_gather | solution.py:62
  159.4 47.7 %all-gather.2 = f32[1024,32]{1,0:T(8,128)S(1)} all-gather(f32[32,32]{1,0:T(8,128)S(1)} %fusion.70), channel_id=4, replica_groups=mesh['tm'=8,'space'=32] {'space'}, dimensions={0}, use_global_device_ids=true | all-gather | bytes 135168 | tf_op jit(solution)/shard_map/all_gather | solution.py:62
  207.3 48.2 %all-gather.3 = f32[1024,32]{1,0:T(8,128)S(1)} all-gather(f32[32,32]{1,0:T(8,128)S(1)} %fusion.73), channel_id=5, replica_groups=mesh['tm'=8,'space'=32] {'space'}, dimensions={0}, use_global_device_ids=true | all-gather | bytes 135168 | tf_op jit(solution)/shard_map/all_gather | solution.py:62
  256.2 2.5 fusion.82
  258.7 47.9 %all-gather.6 = f32[1024,32]{1,0:T(8,128)S(1)} all-gather(f32[32,32]{1,0:T(8,128)S(1)} %fusion.82), channel_id=8, replica_groups=mesh['tm'=8,'space'=32] {'space'}, dimensions={0}, use_global_device_ids=true | all-gather | bytes 135168 | tf_op jit(solution)/shard_map/all_gather | solution.py:62
  308.7 3.7 collective-permute-start.1
  315.2 2.4 collective-permute-done.1
  318.9 2.2 fusion.42
  322.3 54.1 %all-gather = f32[1024,32]{1,0:T(8,128)} all-gather(f32[32,32]{1,0:T(8,128)S(1)} %fusion.64), channel_id=2, replica_groups=mesh['tm'=8,'space'=32] {'space'}, dimensions={0}, use_global_device_ids=true | all-gather | bytes 135168 | tf_op jit(solution)/shard_map/all_gather | solution.py:62
  378.7 47.7 %all-gather.4 = f32[1024,32]{1,0:T(8,128)S(1)} all-gather(f32[32,32]{1,0:T(8,128)S(1)} %fusion.76), channel_id=6, replica_groups=mesh['tm'=8,'space'=32] {'space'}, dimensions={0}, use_global_device_ids=true | all-gather | bytes 135168 | tf_op jit(solution)/shard_map/all_gather | solution.py:62
  427.7 47.8 %all-gather.5 = f32[1024,32]{1,0:T(8,128)S(1)} all-gather(f32[32,32]{1,0:T(8,128)S(1)} %fusion.79), channel_id=7, replica_groups=mesh['tm'=8,'space'=32] {'space'}, dimensions={0}, use_global_device_ids=true | all-gather | bytes 135168 | tf_op jit(solution)/shard_map/all_gather | solution.py:62
  475.8 2.1 gather_fusion
  477.9 2.3 gather_fusion.1
  480.4 2.8 fusion.85
  483.2 66.1 %all-reduce.10.cloned.1.call-done = f32[561,561]{0,1:T(8,128)} async-done(((f32[561,561]{0,1:T(8,128)}), f32[561,561]{0,1:T(8,128)}) %all-reduce.10.cloned.1.call-update) | async-done | bytes 1258900 | tf_op jit(solution)/shard_map/psum | solution.py:67
  549.4 2.6 broadcast_multiply_fusion
  551.9 3.1 copy.49
  557.7 11.7 %cholesky.134 = f32[128,128]{1,0:T(8,128)S(1)} custom-call(f32[128,128]{1,0:T(8,128)S(1)} %cholesky.346), custom_call_target="Cholesky" | custom-call | tf_op jit(solution)/shard_map/jit(cholesky)/cholesky | solution.py:68
  569.5 9.8 %custom-call.35 = f32[1,128,128]{1,2,0:T(8,128)S(1)} custom-call(f32[1,128,128]{2,1,0:T(8,128)S(1)} %get-tuple-element.45), custom_call_target="InvertDiagBlocksLowerTriangular" | custom-call | tf_op jit(solution)/shard_map/jit(cholesky)/cholesky | solution.py:68
  582.3 12.1 %cholesky.274 = f32[128,128]{1,0:T(8,128)S(1)} custom-call(f32[128,128]{1,0:T(8,128)S(1)} %cholesky.350), custom_call_target="Cholesky" | custom-call | tf_op jit(solution)/shard_map/jit(cholesky)/cholesky | solution.py:68
  595.7 9.8 %custom-call.36 = f32[1,128,128]{1,2,0:T(8,128)S(1)} custom-call(f32[1,128,128]{2,1,0:T(8,128)S(1)} %get-tuple-element.42), custom_call_target="InvertDiagBlocksLowerTriangular" | custom-call | tf_op jit(solution)/shard_map/jit(cholesky)/cholesky | solution.py:68
  607.3 11.7 %cholesky.295 = f32[128,128]{1,0:T(8,128)S(1)} custom-call(f32[128,128]{1,0:T(8,128)S(1)} %cholesky.355), custom_call_target="Cholesky" | custom-call | tf_op jit(solution)/shard_map/jit(cholesky)/cholesky | solution.py:68
  619.7 9.8 %custom-call.37 = f32[1,128,128]{1,2,0:T(8,128)S(1)} custom-call(f32[1,128,128]{2,1,0:T(8,128)S(1)} %get-tuple-element.39), custom_call_target="InvertDiagBlocksLowerTriangular" | custom-call | tf_op jit(solution)/shard_map/jit(cholesky)/cholesky | solution.py:68
  631.3 11.9 %cholesky.314 = f32[128,128]{1,0:T(8,128)S(1)} custom-call(f32[128,128]{1,0:T(8,128)S(1)} %cholesky.360), custom_call_target="Cholesky" | custom-call | tf_op jit(solution)/shard_map/jit(cholesky)/cholesky | solution.py:68
  643.8 9.8 %custom-call.38 = f32[1,128,128]{1,2,0:T(8,128)S(1)} custom-call(f32[1,128,128]{2,1,0:T(8,128)S(1)} %get-tuple-element.36), custom_call_target="InvertDiagBlocksLowerTriangular" | custom-call | tf_op jit(solution)/shard_map/jit(cholesky)/cholesky | solution.py:68
  654.8 4.5 cholesky.334
  664.3 3.0 copy.50
  (135 shorter events, 49.2 us)
Async XLA Ops:
  7.2 96.7 %copy-start = (bf16[32,5,2,8,128]{4,3,2,1,0:T(8,128)(2,1)S(1)}, bf16[32,5,2,8,128]{4,3,2,1,0:T(8,128)(2,1)}, u32[]{:S(2)}) copy-start(bf16[32,5,2,8,128]{4,3,2,1,0:T(8,128)(2,1)} %param.12) | copy-start | bytes 1966084
  7.2 542.2 %all-reduce.10.cloned.1.call-start = ((), (), s32[]{:S(2)}) async-start(), calls=%async_computation | async-start | bytes 2908160 | tf_op jit(solution)/shard_map/psum | solution.py:67
  11.5 0.9 copy-start.6
  13.4 49.3 %collective-permute-start.2 = (bf16[32,5,1,8,128]{4,3,2,1,0:T(8,128)(2,1)}, bf16[32,5,1,8,128]{4,3,2,1,0:T(8,128)(2,1)}, u32[]{:S(2)}, u32[]{:S(2)}) collective-permute-start(bf16[32,5,1,8,128]{4,3,2,1,0:T(8,128)(2,1)} %get-tuple-element.31), channel_id=1, source_target_pairs={{0,1},{1,2},{2,3},{3,4},{4,5},{5,6},{6,7},{7,8},{8,9},{9,10},{10,1... | collective-permute-start | bytes 983048 | tf_op jit(solution)/shard_map/ppermute | solution.py:15
  17.2 51.5 %collective-permute-start.3 = (bf16[32,5,1,8,128]{4,3,2,1,0:T(8,128)(2,1)}, bf16[32,5,1,8,128]{4,3,2,1,0:T(8,128)(2,1)}, u32[]{:S(2)}, u32[]{:S(2)}) collective-permute-start(bf16[32,5,1,8,128]{4,3,2,1,0:T(8,128)(2,1)} %get-tuple-element.32), channel_id=1, source_target_pairs={{1,0},{2,1},{3,2},{4,3},{5,4},{6,5},{7,6},{8,7},{9,8},{10,9},{11,1... | collective-permute-start | bytes 983048 | tf_op jit(solution)/shard_map/ppermute | solution.py:18
  26.2 0.8 copy-start.2
  28.1 44.2 %collective-permute-start.4 = (bf16[32,5,1,8,128]{4,3,2,1,0:T(8,128)(2,1)}, bf16[32,5,1,8,128]{4,3,2,1,0:T(8,128)(2,1)}, u32[]{:S(2)}, u32[]{:S(2)}) collective-permute-start(bf16[32,5,1,8,128]{4,3,2,1,0:T(8,128)(2,1)} %get-tuple-element.29), channel_id=1, source_target_pairs={{0,1},{1,2},{2,3},{3,4},{4,5},{5,6},{6,7},{7,8},{8,9},{9,10},{10,1... | collective-permute-start | bytes 983048 | tf_op jit(solution)/shard_map/ppermute | solution.py:15
  30.0 48.3 %collective-permute-start.5 = (bf16[32,5,1,8,128]{4,3,2,1,0:T(8,128)(2,1)}, bf16[32,5,1,8,128]{4,3,2,1,0:T(8,128)(2,1)}, u32[]{:S(2)}, u32[]{:S(2)}) collective-permute-start(bf16[32,5,1,8,128]{4,3,2,1,0:T(8,128)(2,1)} %get-tuple-element.30), channel_id=1, source_target_pairs={{1,0},{2,1},{3,2},{4,3},{5,4},{6,5},{7,6},{8,7},{9,8},{10,9},{11,1... | collective-permute-start | bytes 983048 | tf_op jit(solution)/shard_map/ppermute | solution.py:18
  39.3 0.8 copy-start.4
  41.1 40.7 %collective-permute-start.6 = (bf16[32,5,1,8,128]{4,3,2,1,0:T(8,128)(2,1)}, bf16[32,5,1,8,128]{4,3,2,1,0:T(8,128)(2,1)}, u32[]{:S(2)}, u32[]{:S(2)}) collective-permute-start(bf16[32,5,1,8,128]{4,3,2,1,0:T(8,128)(2,1)} %get-tuple-element.27), channel_id=1, source_target_pairs={{0,1},{1,2},{2,3},{3,4},{4,5},{5,6},{6,7},{7,8},{8,9},{9,10},{10,1... | collective-permute-start | bytes 983048 | tf_op jit(solution)/shard_map/ppermute | solution.py:15
  59.7 2.3 copy-start.20
  59.7 2.3 copy-start.21
  59.7 2.9 copy-start.14
  59.7 9.0 %copy-start.15 = (bf16[32,5,1,8,128]{4,3,2,1,0:T(8,128)(2,1)S(1)}, bf16[32,5,1,8,128]{4,3,2,1,0:T(8,128)(2,1)}, u32[]{:S(2)}) copy-start(bf16[32,5,1,8,128]{4,3,2,1,0:T(8,128)(2,1)} %get-tuple-element.21) | copy-start | bytes 983044
  59.7 11.1 %copy-start.7 = (bf16[32,5,2,8,128]{4,3,2,1,0:T(8,128)(2,1)S(1)}, bf16[32,5,2,8,128]{4,3,2,1,0:T(8,128)(2,1)}, u32[]{:S(2)}) copy-start(bf16[32,5,2,8,128]{4,3,2,1,0:T(8,128)(2,1)} %copy-done.6) | copy-start | bytes 1966084
  62.7 25.2 %collective-permute-start.7 = (bf16[32,5,1,8,128]{4,3,2,1,0:T(8,128)(2,1)S(1)}, bf16[32,5,1,8,128]{4,3,2,1,0:T(8,128)(2,1)S(1)}, u32[]{:S(2)}, u32[]{:S(2)}) collective-permute-start(bf16[32,5,1,8,128]{4,3,2,1,0:T(8,128)(2,1)S(1)} %copy-done.14), channel_id=1, source_target_pairs={{1,0},{2,1},{3,2},{4,3},{5,4},{6,5},{7,6},{8,7},{9,8},{10,9},{11,1... | collective-permute-start | bytes 983048 | tf_op jit(solution)/shard_map/ppermute | solution.py:18
  68.7 3.5 copy-start.13
  68.7 11.6 %copy-start.3 = (bf16[32,5,2,8,128]{4,3,2,1,0:T(8,128)(2,1)S(1)}, bf16[32,5,2,8,128]{4,3,2,1,0:T(8,128)(2,1)}, u32[]{:S(2)}) copy-start(bf16[32,5,2,8,128]{4,3,2,1,0:T(8,128)(2,1)} %copy-done.2) | copy-start | bytes 1966084
  68.8 22.4 %collective-permute-start.12 = (bf16[32,5,1,8,128]{4,3,2,1,0:T(8,128)(2,1)S(1)}, bf16[32,5,1,8,128]{4,3,2,1,0:T(8,128)(2,1)S(1)}, u32[]{:S(2)}, u32[]{:S(2)}) collective-permute-start(bf16[32,5,1,8,128]{4,3,2,1,0:T(8,128)(2,1)S(1)} %copy-done.15), channel_id=1, source_target_pairs={{0,1},{1,2},{2,3},{3,4},{4,5},{5,6},{6,7},{7,8},{8,9},{9,10},{10,1... | collective-permute-start | bytes 983048 | tf_op jit(solution)/shard_map/ppermute | solution.py:15
  72.3 24.9 %collective-permute-start.13 = (bf16[32,5,1,8,128]{4,3,2,1,0:T(8,128)(2,1)S(1)}, bf16[32,5,1,8,128]{4,3,2,1,0:T(8,128)(2,1)S(1)}, u32[]{:S(2)}, u32[]{:S(2)}) collective-permute-start(bf16[32,5,1,8,128]{4,3,2,1,0:T(8,128)(2,1)S(1)} %copy-done.13), channel_id=1, source_target_pairs={{1,0},{2,1},{3,2},{4,3},{5,4},{6,5},{7,6},{8,7},{9,8},{10,9},{11,1... | collective-permute-start | bytes 983048 | tf_op jit(solution)/shard_map/ppermute | solution.py:18
  78.3 11.5 %copy-start.5 = (bf16[32,5,2,8,128]{4,3,2,1,0:T(8,128)(2,1)S(1)}, bf16[32,5,2,8,128]{4,3,2,1,0:T(8,128)(2,1)}, u32[]{:S(2)}) copy-start(bf16[32,5,2,8,128]{4,3,2,1,0:T(8,128)(2,1)} %copy-done.4) | copy-start | bytes 1966084
  78.3 230.3 %collective-permute-start.8 = (bf16[32,5,1,8,128]{4,3,2,1,0:T(8,128)(2,1)}, bf16[32,5,1,8,128]{4,3,2,1,0:T(8,128)(2,1)}, u32[]{:S(2)}, u32[]{:S(2)}) collective-permute-start(bf16[32,5,1,8,128]{4,3,2,1,0:T(8,128)(2,1)} %get-tuple-element.25), channel_id=1, source_target_pairs={{0,1},{1,2},{2,3},{3,4},{4,5},{5,6},{6,7},{7,8},{8,9},{9,10},{10,1... | collective-permute-start | bytes 983048 | tf_op jit(solution)/shard_map/ppermute | solution.py:15
  81.8 230.5 %collective-permute-start.9 = (bf16[32,5,1,8,128]{4,3,2,1,0:T(8,128)(2,1)}, bf16[32,5,1,8,128]{4,3,2,1,0:T(8,128)(2,1)}, u32[]{:S(2)}, u32[]{:S(2)}) collective-permute-start(bf16[32,5,1,8,128]{4,3,2,1,0:T(8,128)(2,1)} %get-tuple-element.26), channel_id=1, source_target_pairs={{1,0},{2,1},{3,2},{4,3},{5,4},{6,5},{7,6},{8,7},{9,8},{10,9},{11,1... | collective-permute-start | bytes 983048 | tf_op jit(solution)/shard_map/ppermute | solution.py:18
  87.9 225.9 %collective-permute-start.10 = (bf16[32,5,1,8,128]{4,3,2,1,0:T(8,128)(2,1)}, bf16[32,5,1,8,128]{4,3,2,1,0:T(8,128)(2,1)}, u32[]{:S(2)}, u32[]{:S(2)}) collective-permute-start(bf16[32,5,1,8,128]{4,3,2,1,0:T(8,128)(2,1)} %get-tuple-element.23), channel_id=1, source_target_pairs={{0,1},{1,2},{2,3},{3,4},{4,5},{5,6},{6,7},{7,8},{8,9},{9,10},{10,1... | collective-permute-start | bytes 983048 | tf_op jit(solution)/shard_map/ppermute | solution.py:15
  91.1 222.7 %collective-permute-start.11 = (bf16[32,5,1,8,128]{4,3,2,1,0:T(8,128)(2,1)}, bf16[32,5,1,8,128]{4,3,2,1,0:T(8,128)(2,1)}, u32[]{:S(2)}, u32[]{:S(2)}) collective-permute-start(bf16[32,5,1,8,128]{4,3,2,1,0:T(8,128)(2,1)} %get-tuple-element.24), channel_id=1, source_target_pairs={{1,0},{2,1},{3,2},{4,3},{5,4},{6,5},{7,6},{8,7},{9,8},{10,9},{11,1... | collective-permute-start | bytes 983048 | tf_op jit(solution)/shard_map/ppermute | solution.py:18
  97.2 2.3 copy-start.16
  97.2 218.0 %collective-permute-start = (bf16[32,5,1,8,128]{4,3,2,1,0:T(8,128)(2,1)}, bf16[32,5,1,8,128]{4,3,2,1,0:T(8,128)(2,1)}, u32[]{:S(2)}, u32[]{:S(2)}) collective-permute-start(bf16[32,5,1,8,128]{4,3,2,1,0:T(8,128)(2,1)} %get-tuple-element.33), channel_id=1, source_target_pairs={{0,1},{1,2},{2,3},{3,4},{4,5},{5,6},{6,7},{7,8},{8,9},{9,10},{10,1... | collective-permute-start | bytes 983048 | tf_op jit(solution)/shard_map/ppermute | solution.py:15
  103.9 2.6 copy-start.10
  106.4 1.3 copy-start.9
  256.2 52.5 %copy-start.12 = (bf16[32,5,1,8,128]{4,3,2,1,0:T(8,128)(2,1)S(1)}, bf16[32,5,1,8,128]{4,3,2,1,0:T(8,128)(2,1)}, u32[]{:S(2)}) copy-start(bf16[32,5,1,8,128]{4,3,2,1,0:T(8,128)(2,1)} %get-tuple-element.34) | copy-start | bytes 983044
  308.7 9.0 %collective-permute-start.1 = (bf16[32,5,1,8,128]{4,3,2,1,0:T(8,128)(2,1)S(1)}, bf16[32,5,1,8,128]{4,3,2,1,0:T(8,128)(2,1)S(1)}, u32[]{:S(2)}, u32[]{:S(2)}) collective-permute-start(bf16[32,5,1,8,128]{4,3,2,1,0:T(8,128)(2,1)S(1)} %copy-done.12), channel_id=1, source_target_pairs={{1,0},{2,1},{3,2},{4,3},{5,4},{6,5},{7,6},{8,7},{9,8},{10,9},{11,1... | collective-permute-start | bytes 983048 | tf_op jit(solution)/shard_map/ppermute | solution.py:18
  426.5 49.1 %copy-start.17 = (f32[32,32]{0,1:T(8,128)S(1)}, f32[32,32]{0,1:T(8,128)}, u32[]{:S(2)}) copy-start(f32[32,32]{0,1:T(8,128)} %copy.44) | copy-start | bytes 12292
  426.5 49.1 %copy-start.18 = (f32[32,32]{0,1:T(8,128)S(1)}, f32[32,32]{0,1:T(8,128)}, u32[]{:S(2)}) copy-start(f32[32,32]{0,1:T(8,128)} %copy.47) | copy-start | bytes 12292
  475.8 4.6 copy-start.1
  475.8 2.2 copy-start.19
  551.9 3.1 copy-start.8
  556.6 1.1 copy-start.11
Sparse Core Ops, SparseCore 0:
  483.3 65.9 all-reduce.9
